TPU v7x, 128 devices: a whole 4x4x4 slice. The times are simulated.
128 devices in a mesh: expert: 32 (over y, x, core), dp: 4 (over z).
Axes of the slice: x: 4, y: 4, z: 4, core: 2. Of those that a mesh axis runs over, the one named last changes fastest.
Arguments:
- tokens: bfloat16 [8192, 3584], P(('expert', 'dp')), may hold values from -6 to 6
- out_grad: bfloat16 [8192, 3584], P(('expert', 'dp')), may hold values from -6 to 6
- route_ids: int32 [8192, 8], P(('expert', 'dp')), may hold values from 0 to 31, all different within a row; in each aligned block of 64 rows (0 to 63, 64 to 127, ...) at most 20 rows name the same one
- route_logits: float32 [8192, 8], P(('expert', 'dp')), may hold values from -6 to 6
- gate_up: bfloat16 [32, 2, 3584, 1024], P('expert', None, None, 'dp'), may hold values from -0.09375 to 0.09375
- down: bfloat16 [32, 1024, 3584], P('expert', 'dp'), may hold values from -0.1875 to 0.1875
- moment1: bfloat16 [32, 1024, 3584], P('expert', 'dp'), may hold values from -8 to 8
- moment2: bfloat16 [32, 1024, 3584], P('expert', 'dp'), may hold values from 0.5 to 20
Outputs:
- token_grad: bfloat16 [8192, 3584], P(('expert', 'dp'))
- router_grad: float32 [8192, 8], P(('expert', 'dp'))
- new_down: bfloat16 [32, 1024, 3584], P('expert', 'dp')
- new_moment1: bfloat16 [32, 1024, 3584], P('expert', 'dp')
- new_moment2: bfloat16 [32, 1024, 3584], P('expert', 'dp')
Inputs may be any that keep to these rules, and one draw needn't show every extreme that they name: `route_ids`: each row names 8 different experts. Within the 64 rows of one device no expert is named more than 20 times, and in every draw the rows of some device name some expert exactly 20 times.
All inputs are finite; a program needn't handle non-finite values.
Results may differ from a plain program's by a relative error of at most 0.012.
Values may be sent and summed in bfloat16 or wider, within the bound.
No kernel may reach another device: no remote copies, remote signals or barrier semaphores. Data moves between devices by JAX's collectives and lax.ppermute only.
A program may use at most 192 MiB of HBM per device.

v0:
```python
import jax
import jax.numpy as jnp
from jax import lax
from jax.sharding import PartitionSpec as P

STEP = 10
ROUTE_SCALE = 2.5
BETA_ONE = 0.9
BETA_TWO = 0.95
LEARN_RATE = 0.001
DECAY = 0.1
EPSILON = 1e-08
LANE = 128
HALVES = 2


def contract_last(left, right):
    return lax.dot_general(
        left, right, (((1,), (1,)), ((), ())), preferred_element_type=jnp.float32
    )


def contract_first(left, right):
    return lax.dot_general(
        left, right, (((0,), (0,)), ((), ())), preferred_element_type=jnp.float32
    )


def shards(tokens, out_grad, route_ids, route_logits, gate_up, down, moment1, moment2):
    experts = lax.axis_size("expert")
    data_ways = lax.axis_size("dp")
    tok_rows, model_width = tokens.shape
    top_count = route_ids.shape[1]
    local_ffw = down.shape[1]
    part_ffw = local_ffw // HALVES
    capacity = min(tok_rows, max(2, 5 * tok_rows * top_count // (4 * experts)))
    capacity = -(-capacity // 8) * 8
    slot_count = experts * capacity
    scores = jax.nn.sigmoid(route_logits)
    score_sum = jnp.sum(scores, axis=1, keepdims=True)
    route_weight = (ROUTE_SCALE * scores / score_sum).astype(jnp.bfloat16)
    flat_ids = route_ids.reshape(-1)
    onehot = (flat_ids[:, None] == jnp.arange(experts, dtype=jnp.int32)[None, :]).astype(jnp.int32)
    before = jnp.cumsum(onehot, axis=0) - onehot
    places = jnp.sum(before * onehot, axis=1)
    slot_index = flat_ids * capacity + places
    matched = (jnp.arange(slot_count, dtype=jnp.int32)[:, None] == slot_index[None, :]).astype(
        jnp.float32
    )
    tok_match = jnp.sum(matched.reshape(slot_count, tok_rows, top_count), axis=2).astype(
        jnp.bfloat16
    )
    send_weight = jnp.sum(matched * route_weight.astype(jnp.float32).reshape(-1)[None, :], axis=1)
    weight_block = jnp.zeros((slot_count, LANE), jnp.float32).at[:, 0].set(send_weight)
    payload = jnp.concatenate([tokens, out_grad], axis=1)
    send_rows = jnp.dot(tok_match, payload, preferred_element_type=jnp.float32)
    send_rows = jnp.concatenate([send_rows, weight_block], axis=1).astype(jnp.bfloat16)
    send_rows = send_rows.reshape(experts, capacity, 2 * model_width + LANE)
    full_down = lax.all_gather(down, "dp", axis=1, tiled=True)[0]
    gu_parts = [
        lax.all_gather(
            gate_up[:, :, :, h * part_ffw : (h + 1) * part_ffw], "dp", axis=3, tiled=True
        )[0]
        for h in range(HALVES)
    ]
    recv_rows = lax.all_to_all(send_rows, "expert", split_axis=0, concat_axis=0, tiled=True)
    recv_rows = recv_rows.reshape(slot_count, 2 * model_width + LANE)
    xs_rows = recv_rows[:, :model_width]
    gs_rows = recv_rows[:, model_width : 2 * model_width]
    slot_weight = recv_rows[:, 2 * model_width].astype(jnp.float32)
    back_full = contract_last(gs_rows, full_down)
    back_full = back_full.reshape(slot_count, data_ways, HALVES, part_ffw)
    scaled = (slot_weight[:, None] * gs_rows.astype(jnp.float32)).astype(jnp.bfloat16)
    grad_parts = []
    affinity = jnp.zeros((slot_count,), jnp.float32)
    route_acc = jnp.zeros((slot_count, model_width), jnp.float32)
    for h in range(HALVES):
        gate_w = gu_parts[h][0]
        up_w = gu_parts[h][1]
        back_raw = back_full[:, :, h, :].reshape(slot_count, data_ways * part_ffw)
        pre_gate = jnp.dot(xs_rows, gate_w, preferred_element_type=jnp.float32)
        pre_up = jnp.dot(xs_rows, up_w, preferred_element_type=jnp.float32)
        sig_gate = jax.nn.sigmoid(pre_gate)
        silu_gate = pre_gate * sig_gate
        hidden = (silu_gate * pre_up).astype(jnp.bfloat16)
        affinity = affinity + jnp.sum(hidden.astype(jnp.float32) * back_raw, axis=1)
        local_grad = contract_first(hidden, scaled)
        grad_parts.append(
            lax.psum_scatter(local_grad.astype(jnp.bfloat16), "dp", scatter_dimension=0, tiled=True)
        )
        back = slot_weight[:, None] * back_raw
        gate_grad = (back * pre_up * sig_gate * (1.0 + pre_gate * (1.0 - sig_gate))).astype(
            jnp.bfloat16
        )
        up_grad = (back * silu_gate).astype(jnp.bfloat16)
        route_acc = route_acc + contract_last(gate_grad, gate_w) + contract_last(up_grad, up_w)
    affinity_block = (
        jnp.zeros((slot_count, LANE), jnp.float32)
        .at[:, 0]
        .set(affinity.astype(jnp.bfloat16).astype(jnp.float32))
    )
    ret_rows = jnp.concatenate(
        [route_acc.astype(jnp.bfloat16).astype(jnp.float32), affinity_block], axis=1
    )
    ret_rows = ret_rows.astype(jnp.bfloat16).reshape(experts, capacity, model_width + LANE)
    back_rows = lax.all_to_all(ret_rows, "expert", split_axis=0, concat_axis=0, tiled=True)
    back_rows = back_rows.reshape(slot_count, model_width + LANE)
    token_grad = contract_first(tok_match, back_rows[:, :model_width]).astype(jnp.bfloat16)
    back_affinity = back_rows[:, model_width].astype(jnp.float32)
    route_affinity = jnp.sum(matched * back_affinity[:, None], axis=0)
    route_affinity = route_affinity.reshape(tok_rows, top_count)
    mixed = jnp.sum(route_affinity * scores, axis=1, keepdims=True) / score_sum
    router_grad = ROUTE_SCALE * scores * (1.0 - scores) * (route_affinity - mixed) / score_sum
    grad_shard = jnp.concatenate(grad_parts, axis=0).astype(jnp.float32)
    down_grad = (grad_shard / data_ways)[None]
    corr_one = 1.0 - BETA_ONE**STEP
    corr_two = 1.0 - BETA_TWO**STEP
    down_wide = down.astype(jnp.float32)
    first = BETA_ONE * moment1.astype(jnp.float32) + (1.0 - BETA_ONE) * down_grad
    second = BETA_TWO * moment2.astype(jnp.float32) + (1.0 - BETA_TWO) * down_grad * down_grad
    update = first / corr_one / (jnp.sqrt(second / corr_two) + EPSILON) + DECAY * down_wide
    new_down = (down_wide - LEARN_RATE * update).astype(jnp.bfloat16)
    return (
        token_grad,
        router_grad,
        new_down,
        first.astype(jnp.bfloat16),
        second.astype(jnp.bfloat16),
    )


def solution(mesh):
    placed = (
        P(("expert", "dp"), None),
        P(("expert", "dp"), None),
        P(("expert", "dp"), None),
        P(("expert", "dp"), None),
        P("expert", None, None, "dp"),
        P("expert", "dp", None),
        P("expert", "dp", None),
        P("expert", "dp", None),
    )
    return jax.shard_map(
        shards,
        mesh=mesh,
        in_specs=placed,
        out_specs=(
            P(("expert", "dp"), None),
            P(("expert", "dp"), None),
            P("expert", "dp", None),
            P("expert", "dp", None),
            P("expert", "dp", None),
        ),
        check_vma=False,
    )
```

profile of v0, /device:TPU:1, one launch (start us, length us, event | category | flops | bytes accessed | tf_op | source)
XLA Modules:
  0.0 411.3 jit_solution(7383616715635387772)
XLA Ops:
  7.2 0.7 all-gather.4.cloned.1.call-update
  8.0 4.2 %fusion.43 = (bf16[1,2,3584,128]{3,2,1,0:T(8,128)(2,1)}, bf16[1,2,3584,128]{3,2,1,0:T(8,128)(2,1)}) fusion(bf16[1,2,3584,256]{3,2,1,0:T(8,128)(2,1)} %param.16), kind=kLoop, calls=%fused_computation.92 | loop fusion | bytes 7340032 | tf_op jit(solution)/shard_map/slice | solution.py:62
  12.3 0.1 eq.50
  12.4 0.1 eq.46
  12.5 1.2 reduce-window.6
  13.7 0.2 slice_reduce_fusion
  14.1 0.1 reshape.225
  14.2 0.1 fusion.36
  14.3 0.1 reduce_sum.75
  14.4 0.6 compare_reduce_fusion
  15.0 0.2 select_reduce_fusion.1
  15.3 0.7 select_convert_fusion.1
  15.9 0.2 reshape.230
  16.2 0.1 copy.46
  16.3 0.5 convert_reduce_fusion
  16.9 3.3 convolution_convert_fusion
  20.1 5.0 %pad_maximum_fusion = bf16[32,24,7296]{2,1,0:T(8,128)(2,1)} fusion(bf16[32,24,128]{2,1,0:T(8,128)(2,1)S(1)} %bitcast.86, bf16[32,24,7168]{2,1,0:T(8,128)(2,1)S(1)} %bitcast.80), kind=kLoop, calls=%fused_computation.1 | loop fusion | flops 22413312 | bytes 22413312 | tf_op jit(solution)/shard_map/concatenate | solution.py:57
  25.1 8.6 %all-to-all-start = ((bf16[32,24,7296]{2,1,0:T(8,128)(2,1)}), bf16[32,24,7296]{2,1,0:T(8,128)(2,1)}, u32[]{:S(2)}, u32[]{:S(2)}) async-start(bf16[32,24,7296]{2,1,0:T(8,128)(2,1)} %pad_maximum_fusion), calls=%async_computation | async-start | bytes 22413312 | tf_op jit(solution)/shard_map/all_to_all | solution.py:66
  33.8 0.7 all-gather.6.cloned.1.call-update
  34.5 0.2 reduce-scatter.5.cloned.1.call-start
  34.7 134.1 %all-to-all-done = bf16[32,24,7296]{2,1,0:T(8,128)(2,1)} async-done(((bf16[32,24,7296]{2,1,0:T(8,128)(2,1)}), bf16[32,24,7296]{2,1,0:T(8,128)(2,1)}, u32[]{:S(2)}, u32[]{:S(2)}) %all-to-all-start) | async-done | bytes 11206688 | tf_op jit(solution)/shard_map/all_to_all | solution.py:66
  168.8 1.1 convert_reduce_fusion.2
  169.9 9.8 %fusion.2 = f32[768,4,2,128]{0,3,2,1:T(8,128)S(1)} fusion(bf16[4,2,128,3584]{3,2,1,0:T(8,128)(2,1)} %bitcast.88, bf16[768,7296]{1,0:T(8,128)(2,1)} %bitcast.3), kind=kOutput, calls=%fused_computation.9 | convolution fusion | flops 5637144576 | bytes 15990784 | tf_op jit(solution)/shard_map/dot_general | solution.py:18
  179.7 0.3 fusion.44
  180.1 7.8 %fusion.14 = f32[768,512]{0,1:T(8,128)S(1)} fusion(bf16[768,7296]{1,0:T(8,128)(2,1)} %bitcast.3, bf16[1,2,3584,512]{3,2,1,0:T(8,128)(2,1)} %all-gather.8.cloned.1.call-done), kind=kOutput, calls=%fused_computation.28 | convolution fusion | flops 2818572288 | bytes 10747904 | tf_op jit(solution)/shard_map/dot_general | solution.py:81
  188.0 7.7 %fusion.27 = (f32[768]{0:T(1024)S(1)}, bf16[768,512]{0,1:T(8,128)(2,1)S(1)}, bf16[768,512]{0,1:T(8,128)(2,1)}, bf16[768,512]{0,1:T(8,128)(2,1)}) fusion(f32[768,4,1,128]{0,3,2,1:T(8,128)S(1)} %get-tuple-element.57, f32[768,512]{0,1:T(8,128)S(1)} %fusion.14, f32[768]{0:T(1024)S(1)} %convert_reduce_fusion.2, bf16[1,2,3584,512]{3,2,1,0:T(8,128)(2,1)S(1)} %copy-done.2, ...), kind=kOutput, calls=%fused_computation.44 | convolution fusion | flops 2826042624 | bytes 14687232 | tf_op jit(solution)/shard_map/dot_general | solution.py:82
  195.6 7.5 %convolution_convert_fusion.1 = bf16[512,3584]{1,0:T(8,128)(2,1)} fusion(bf16[768,512]{0,1:T(8,128)(2,1)S(1)} %get-tuple-element.45, f32[768]{0:T(1024)S(1)} %convert_reduce_fusion.2, bf16[768,7296]{1,0:T(8,128)(2,1)} %bitcast.3), kind=kOutput, calls=%fused_computation.4 | convolution fusion | flops 2828664832 | bytes 9964544 | tf_op jit(solution)/shard_map/dot_general | solution.py:24
  203.2 0.3 reduce-scatter.3.cloned.1.call-start
  203.5 44.5 %all-gather.6.cloned.1.call-done = bf16[1,2,3584,512]{3,2,1,0:T(8,128)(2,1)} async-done(((bf16[1,2,3584,128]{3,2,1,0:T(8,128)(2,1)}), bf16[1,2,3584,512]{3,2,1,0:T(8,128)(2,1)}) %all-gather.6.cloned.1.call-update) | async-done | bytes 7340048 | tf_op jit(solution)/shard_map/all_gather | solution.py:61
  248.0 6.9 %fusion.18 = f32[768,512]{0,1:T(8,128)S(1)} fusion(bf16[768,7296]{1,0:T(8,128)(2,1)} %bitcast.3, bf16[1,2,3584,512]{3,2,1,0:T(8,128)(2,1)} %all-gather.6.cloned.1.call-done), kind=kOutput, calls=%fused_computation.32 | convolution fusion | flops 2818572288 | bytes 10747904 | tf_op jit(solution)/shard_map/dot_general | solution.py:81
  254.9 7.6 %fusion.28 = (f32[768]{0:T(1024)S(1)}, bf16[768,512]{0,1:T(8,128)(2,1)S(1)}, bf16[768,512]{0,1:T(8,128)(2,1)}, bf16[768,512]{0,1:T(8,128)(2,1)}) fusion(f32[768,4,1,128]{0,3,2,1:T(8,128)S(1)} %get-tuple-element.58, f32[768,512]{0,1:T(8,128)S(1)} %fusion.18, f32[768]{0:T(1024)S(1)} %convert_reduce_fusion.2, bf16[1,2,3584,512]{3,2,1,0:T(8,128)(2,1)S(1)} %copy-done.8, ...), kind=kOutput, calls=%fused_computation.47 | convolution fusion | flops 2826042624 | bytes 14687232 | tf_op jit(solution)/shard_map/dot_general | solution.py:82
  262.5 7.5 %convolution_convert_fusion.2 = bf16[512,3584]{1,0:T(8,128)(2,1)} fusion(bf16[768,512]{0,1:T(8,128)(2,1)S(1)} %get-tuple-element.47, f32[768]{0:T(1024)S(1)} %convert_reduce_fusion.2, bf16[768,7296]{1,0:T(8,128)(2,1)} %bitcast.3), kind=kOutput, calls=%fused_computation.5 | convolution fusion | flops 2828664832 | bytes 9964544 | tf_op jit(solution)/shard_map/dot_general | solution.py:24
  270.1 1.1 copy-done.9
  271.2 8.2 %fusion.24 = f32[768,3584]{1,0:T(8,128)} fusion(bf16[768,512]{0,1:T(8,128)(2,1)S(1)} %copy-done.9, bf16[1,2,3584,512]{3,2,1,0:T(8,128)(2,1)} %all-gather.8.cloned.1.call-done), kind=kOutput, calls=%fused_computation.38 | convolution fusion | flops 2818572288 | bytes 15466496 | tf_op jit(solution)/shard_map/dot_general | solution.py:18
  279.3 8.1 %fusion.22 = f32[768,3584]{1,0:T(8,128)} fusion(bf16[768,512]{0,1:T(8,128)(2,1)S(1)} %copy-done.11, bf16[1,2,3584,512]{3,2,1,0:T(8,128)(2,1)} %all-gather.6.cloned.1.call-done), kind=kOutput, calls=%fused_computation.36 | convolution fusion | flops 2818572288 | bytes 15466496 | tf_op jit(solution)/shard_map/dot_general | solution.py:18
  287.4 5.8 %fusion.23 = f32[768,3584]{1,0:T(8,128)} fusion(bf16[768,512]{0,1:T(8,128)(2,1)S(1)} %copy-done.10, bf16[1,2,3584,512]{3,2,1,0:T(8,128)(2,1)S(1)} %bitcast.90), kind=kOutput, calls=%fused_computation.37 | convolution fusion | flops 2818572288 | bytes 15466496 | tf_op jit(solution)/shard_map/dot_general | solution.py:18
  293.2 15.9 %add_convert_fusion = bf16[768,3584]{1,0:T(8,128)(2,1)} fusion(f32[768,3584]{1,0:T(8,128)} %fusion.24, f32[768,3584]{1,0:T(8,128)} %fusion.23, f32[768,3584]{1,0:T(8,128)} %fusion.22, bf16[768,512]{0,1:T(8,128)(2,1)S(1)} %copy-done.3, bf16[1,2,3584,512]{3,2,1,0:T(8,128)(2,1)} %all-gather.8.cloned.1.call-done), kind=kOutput, calls=%fused_computation.3 | convolution fusion | flops 2829582336 | bytes 42991616 | tf_op jit(solution)/shard_map/dot_general | solution.py:18
  309.2 0.6 select_convert_fusion
  309.8 0.2 reshape.232
  310.1 3.0 pad_maximum_fusion.1
  313.0 75.7 %all_to_all.10 = bf16[32,24,3712]{2,1,0:T(8,128)(2,1)S(1)} all-to-all(bf16[32,24,3712]{2,1,0:T(8,128)(2,1)S(1)} %pad_maximum_fusion.1), channel_id=1, replica_groups=mesh['expert'=32,'dp'=4] {'expert'}, dimensions={0} | all-to-all | bytes 11403264 | tf_op jit(solution)/shard_map/all_to_all | solution.py:106
  388.8 2.5 copy-done.1
  391.3 0.1 convert_reduce_fusion.1
  391.5 0.3 select_reduce_fusion
  391.7 0.1 reshape.224
  391.9 0.6 multiply_divide_fusion
  392.6 4.4 %fusion.5 = bf16[64,3584]{1,0:T(8,128)(2,1)} fusion(bf16[768,3712]{1,0:T(8,128)(2,1)} %bitcast.83, bf16[768,64]{0,1:T(8,128)(2,1)S(1)} %convert_reduce_fusion), kind=kOutput, calls=%fused_computation.15 | convolution fusion | flops 352550912 | bytes 6062080 | tf_op jit(solution)/shard_map/dot_general | solution.py:24
  397.0 7.8 %fusion.26 = (bf16[1,256,3584]{2,1,0:T(8,128)(2,1)}, bf16[1,256,3584]{2,1,0:T(8,128)(2,1)}, bf16[1,256,3584]{2,1,0:T(8,128)(2,1)}) fusion(bf16[1,256,3584]{2,1,0:T(8,128)(2,1)} %param.19, bf16[1,128,3584]{2,1,0:T(8,128)(2,1)} %bitcast.84, bf16[1,128,3584]{2,1,0:T(8,128)(2,1)} %bitcast.85, bf16[1,256,3584]{2,1,0:T(8,128)(2,1)} %param.18, ...), kind=kLoop, calls=%fused_computation.40 | loop fusion | flops 23855104 | bytes 12845056 | tf_op jit(solution)/shard_map/convert_element_type | solution.py:128
  (52 shorter events, 0.8 us)
Async XLA Ops:
  7.2 162.7 %all-gather.4.cloned.1.call-start = ((), (), s32[]{:S(2)}) async-start(), calls=%async_computation.4 | async-start | bytes 9175040 | tf_op jit(solution)/shard_map/all_gather | solution.py:59
  7.9 4.3 %copy-start.7 = (s32[64,8]{0,1:T(8,128)S(1)}, s32[64,8]{0,1:T(8,128)}, u32[]{:S(2)}) copy-start(s32[64,8]{0,1:T(8,128)} %param.14) | copy-start | bytes 6148
  7.9 6.0 %copy-start.6 = (f32[64,8]{0,1:T(8,128)S(1)}, f32[64,8]{0,1:T(8,128)}, u32[]{:S(2)}) copy-start(f32[64,8]{0,1:T(8,128)} %param.15) | copy-start | bytes 6148
  7.9 8.9 %copy-start.4 = (bf16[64,3584]{1,0:T(8,128)(2,1)S(1)}, bf16[64,3584]{1,0:T(8,128)(2,1)}, u32[]{:S(2)}) copy-start(bf16[64,3584]{1,0:T(8,128)(2,1)} %param.13) | copy-start | bytes 1376260
  7.9 8.9 %copy-start.5 = (bf16[64,3584]{1,0:T(8,128)(2,1)S(1)}, bf16[64,3584]{1,0:T(8,128)(2,1)}, u32[]{:S(2)}) copy-start(bf16[64,3584]{1,0:T(8,128)(2,1)} %param.12) | copy-start | bytes 1376260
  7.9 172.1 %all-gather.8.cloned.1.call-start = ((), (), s32[]{:S(2)}) async-start(), calls=%async_computation.6 | async-start | bytes 9175040 | tf_op jit(solution)/shard_map/all_gather | solution.py:61
  25.1 143.7 %all-to-all-start = ((bf16[32,24,7296]{2,1,0:T(8,128)(2,1)}), bf16[32,24,7296]{2,1,0:T(8,128)(2,1)}, u32[]{:S(2)}, u32[]{:S(2)}) async-start(bf16[32,24,7296]{2,1,0:T(8,128)(2,1)} %pad_maximum_fusion), calls=%async_computation | async-start | bytes 22413312 | tf_op jit(solution)/shard_map/all_to_all | solution.py:66
  33.8 214.2 %all-gather.6.cloned.1.call-start = ((), (), s32[]{:S(2)}) async-start(), calls=%async_computation.5 | async-start | bytes 9175040 | tf_op jit(solution)/shard_map/all_gather | solution.py:61
  34.5 362.5 %reduce-scatter.5.cloned.1.call-start = ((), (), s32[]{:S(2)}) async-start(), calls=%async_computation.8 | async-start | bytes 4587520 | tf_op jit(solution)/shard_map/reduce_scatter | solution.py:89
  180.1 7.9 %copy-start.2 = (bf16[1,2,3584,512]{3,2,1,0:T(8,128)(2,1)S(1)}, bf16[1,2,3584,512]{3,2,1,0:T(8,128)(2,1)}, u32[]{:S(2)}) copy-start(bf16[1,2,3584,512]{3,2,1,0:T(8,128)(2,1)} %all-gather.8.cloned.1.call-done) | copy-start | bytes 22020100
  203.2 193.8 %reduce-scatter.3.cloned.1.call-start = ((), (), s32[]{:S(2)}) async-start(), calls=%async_computation.7 | async-start | bytes 4587520 | tf_op jit(solution)/shard_map/reduce_scatter | solution.py:89
  248.0 6.9 %copy-start.8 = (bf16[1,2,3584,512]{3,2,1,0:T(8,128)(2,1)S(1)}, bf16[1,2,3584,512]{3,2,1,0:T(8,128)(2,1)}, u32[]{:S(2)}) copy-start(bf16[1,2,3584,512]{3,2,1,0:T(8,128)(2,1)} %all-gather.6.cloned.1.call-done) | copy-start | bytes 22020100
  270.0 1.1 copy-start.9
  271.2 8.2 %copy-start.11 = (bf16[768,512]{0,1:T(8,128)(2,1)S(1)}, bf16[768,512]{0,1:T(8,128)(2,1)}, u32[]{:S(2)}) copy-start(bf16[768,512]{0,1:T(8,128)(2,1)} %get-tuple-element.56) | copy-start | bytes 2359300
  271.2 16.2 %slice-start = ((s8[7340032]{0:T(1024)(128)(4,1)}), s8[4194304]{0:T(1024)(128)(4,1)S(1)}, s32[]{:S(2)}) async-start(s8[7340032]{0:T(1024)(128)(4,1)} %bitcast.89), calls=%async_computation.9 | async-start | bytes 8388608
  279.3 8.1 %slice-start.1 = ((s8[7340032]{0:T(1024)(128)(4,1)}), s8[3145728]{0:T(1024)(128)(4,1)S(1)}, s32[]{:S(2)}) async-start(s8[7340032]{0:T(1024)(128)(4,1)} %bitcast.89), calls=%async_computation.10 | async-start | bytes 6291456
  279.3 8.1 %copy-start.10 = (bf16[768,512]{0,1:T(8,128)(2,1)S(1)}, bf16[768,512]{0,1:T(8,128)(2,1)}, u32[]{:S(2)}) copy-start(bf16[768,512]{0,1:T(8,128)(2,1)} %get-tuple-element.48) | copy-start | bytes 2359300
  287.4 5.8 %copy-start.3 = (bf16[768,512]{0,1:T(8,128)(2,1)S(1)}, bf16[768,512]{0,1:T(8,128)(2,1)}, u32[]{:S(2)}) copy-start(bf16[768,512]{0,1:T(8,128)(2,1)} %get-tuple-element.55) | copy-start | bytes 2359300
  388.8 2.6 copy-start.1
  388.8 8.2 %copy-start = (bf16[1,256,3584]{2,1,0:T(8,128)(2,1)S(1)}, bf16[1,256,3584]{2,1,0:T(8,128)(2,1)}, u32[]{:S(2)}) copy-start(bf16[1,256,3584]{2,1,0:T(8,128)(2,1)} %param.17) | copy-start | bytes 5505028
Sparse Core Ops, SparseCore 0:
  9.6 77.5 all-gather.3
  89.5 77.6 all-gather.7
  169.4 78.5 all-gather.5
  250.3 44.3 reduce-scatter.4
  297.0 42.3 reduce-scatter.2
where the time goes:
time: 412 us; the launch traced here: 411 us
  waiting for transfers between devices  180 us (44%)
  matrix products  101 us (25%)
  blocking collectives  75.7 us (18%)
  other arithmetic  22 us (5%)
  between operations  14.1 us (3%)
  local copies, waits for them, and re-layouts  9.74 us (2%)
  starting transfers between devices  9.23 us (2%)
    all_to_all x1, waiting for transfers between devices, shards(): lax.all_to_all(send_rows, 'expert', split_axis=0, concat_axis=0, tiled=True)  134 us
    all_to_all x1, blocking collectives, shards(): lax.all_to_all(ret_rows, 'expert', split_axis=0, concat_axis=0, tiled=True)  75.7 us
    dot_general x5, matrix products, contract_last(): lax.dot_general(left, right, (((1,), (1,)), ((), ())), preferred_element_...  47.8 us
    all_gather x2, waiting for transfers between devices, shards(): lax.all_gather(gate_up[:, :, :, h * part_ffw:(h + 1) * part_ffw], 'dp', a...  44.5 us
    dot_general x3, matrix products, contract_first(): lax.dot_general(left, right, (((0,), (0,)), ((), ())), preferred_element_...  19.4 us
    dot_general x2, matrix products, shards(): pre_up = jnp.dot(xs_rows, up_w, preferred_element_type=jnp.float32)  15.3 us
    dot_general x2, matrix products, shards(): pre_gate = jnp.dot(xs_rows, gate_w, preferred_element_type=jnp.float32)  14.8 us
    all_to_all x1, starting transfers between devices, shards(): lax.all_to_all(send_rows, 'expert', split_axis=0, concat_axis=0, tiled=True)  8.63 us
  transfers between devices with their start and end apart: 6, of which 2 were waited for; matrix products, arithmetic and copies ran while one was open for 29% of the time, Pallas kernels for 0%

commit v1 on v0

--- a/solution.py
+++ b/solution.py
@@ -12,6 +12,22 @@
 EPSILON = 1e-08
 LANE = 128
 HALVES = 2
+
+
+def collect(x, axis, dim):
+    ways, here, step = (lax.axis_size(axis), lax.axis_index(axis), x.shape[dim])
+    dims = [n * ways if d == dim else n for d, n in enumerate(x.shape)]
+    full = lax.dynamic_update_slice_in_dim(jnp.zeros(dims, x.dtype), x, here * step, axis=dim)
+    going_up = going_down = x
+    for far in range(1, ways // 2 + 1):
+        going_up = lax.ppermute(going_up, axis, [(d, (d + 1) % ways) for d in range(ways)])
+        full = lax.dynamic_update_slice_in_dim(full, going_up, (here - far) % ways * step, axis=dim)
+        if 2 * far < ways:
+            going_down = lax.ppermute(going_down, axis, [(d, (d - 1) % ways) for d in range(ways)])
+            full = lax.dynamic_update_slice_in_dim(
+                full, going_down, (here + far) % ways * step, axis=dim
+            )
+    return full
 
 
 def contract_last(left, right):
@@ -58,9 +74,7 @@
     send_rows = send_rows.reshape(experts, capacity, 2 * model_width + LANE)
     full_down = lax.all_gather(down, "dp", axis=1, tiled=True)[0]
     gu_parts = [
-        lax.all_gather(
-            gate_up[:, :, :, h * part_ffw : (h + 1) * part_ffw], "dp", axis=3, tiled=True
-        )[0]
+        collect(gate_up[:, :, :, h * part_ffw : (h + 1) * part_ffw], "dp", 3)[0]
         for h in range(HALVES)
     ]
     recv_rows = lax.all_to_all(send_rows, "expert", split_axis=0, concat_axis=0, tiled=True)

time: 412 us -> 433 us (1.051); the launches traced: 411 us -> 426 us
  local copies, waits for them, and re-layouts: 9.74 us -> 33.4 us
  waiting for transfers between devices: 180 us -> 163 us
  starting transfers between devices: 9.23 us -> 15.9 us
    ppermute x0 -> x6, waiting for transfers between devices: none -> 162 us  [the longest x4 162 us: collect(): lax.ppermute(going_up, axis, [(d, (d + 1) % ways) for d in range(ways)])]
    all_to_all x1, waiting for transfers between devices: 134 us -> 0.01 us  [shards(): lax.all_to_all(send_rows, 'expert', split_axis=0, concat_axis=0, tiled=True)]
    all_gather x2 -> x0, waiting for transfers between devices: 44.5 us -> none  [shards(): lax.all_gather(gate_up[:, :, :, h * part_ffw:(h + 1) * part_ffw], 'dp', a...]
    dynamic_update_slice x0 -> x8, local copies, waits for them, and re-layouts: none -> 18 us  [the longest x4 10.3 us: collect(): lax.dynamic_update_slice_in_dim(full, going_up, (here - far) % ways * ste...]
    ppermute x0 -> x6, starting transfers between devices: none -> 6.95 us  [the longest x2 4.8 us: collect(): lax.ppermute(going_down, axis, [(d, (d - 1) % ways) for d in range(ways)])]
    squeeze x0 -> x2, local copies, waits for them, and re-layouts: none -> 4.61 us  [shards(): collect(gate_up[:, :, :, h * part_ffw:(h + 1) * part_ffw], 'dp', 3)[0]]
  transfers between devices with their start and end apart: 6 -> 10, of which waited for: 2 -> 3; matrix products, arithmetic and copies ran while one was open for 29% -> 30% of each run, Pallas kernels for 0% -> 0%
where the time goes in v1:
time: 433 us; the launch traced here: 426 us
  waiting for transfers between devices  163 us (38%)
  matrix products  101 us (23%)
  blocking collectives  74.9 us (17%)
  local copies, waits for them, and re-layouts  33.4 us (8%)
  other arithmetic  23.9 us (6%)
  starting transfers between devices  15.9 us (4%)
  between operations  14.2 us (3%)
    ppermute x4, waiting for transfers between devices, collect(): lax.ppermute(going_up, axis, [(d, (d + 1) % ways) for d in range(ways)])  162 us
    all_to_all x1, blocking collectives, shards(): lax.all_to_all(ret_rows, 'expert', split_axis=0, concat_axis=0, tiled=True)  74.9 us
    dot_general x5, matrix products, contract_last(): lax.dot_general(left, right, (((1,), (1,)), ((), ())), preferred_element_...  46.1 us
    dot_general x3, matrix products, contract_first(): lax.dot_general(left, right, (((0,), (0,)), ((), ())), preferred_element_...  19.6 us
    dot_general x2, matrix products, shards(): pre_gate = jnp.dot(xs_rows, gate_w, preferred_element_type=jnp.float32)  15.4 us
    dot_general x2, matrix products, shards(): pre_up = jnp.dot(xs_rows, up_w, preferred_element_type=jnp.float32)  15.1 us
    dynamic_update_slice x4, local copies, waits for them, and re-layouts, collect(): lax.dynamic_update_slice_in_dim(full, going_up, (here - far) % ways * ste...  10.3 us
  transfers between devices with their start and end apart: 10, of which 3 were waited for; matrix products, arithmetic and copies ran while one was open for 30% of the time, Pallas kernels for 0%

profile of v1, /device:TPU:1, one launch (start us, length us, event | category | flops | bytes accessed | tf_op | source)
XLA Modules:
  0.0 426.1 jit_solution(13890575310525948265)
XLA Ops:
  7.2 0.8 copy.42
  8.1 0.6 compare_reduce_fusion
  8.8 1.2 reduce-window.6
  10.4 0.7 fusion.42
  11.1 0.7 fusion.40
  12.3 0.7 select_convert_fusion.1
  13.2 0.7 multiply_add_fusion
  13.9 0.5 convert_reduce_fusion
  14.5 4.5 %convolution_convert_fusion = bf16[768,7168]{1,0:T(8,128)(2,1)S(1)} fusion(bf16[64,3584]{1,0:T(8,128)(2,1)} %param.13, bf16[64,3584]{1,0:T(8,128)(2,1)} %param.12, bf16[768,64]{0,1:T(8,128)(2,1)S(1)} %convert_reduce_fusion), kind=kOutput, calls=%fused_computation | convolution fusion | flops 711983104 | bytes 12025856 | tf_op jit(solution)/shard_map/dot_general | solution.py:72
  19.0 4.8 %pad_maximum_fusion = bf16[32,24,7296]{2,1,0:T(8,128)(2,1)} fusion(bf16[32,24,128]{2,1,0:T(8,128)(2,1)S(1)} %bitcast.102, bf16[32,24,7168]{2,1,0:T(8,128)(2,1)S(1)} %bitcast.96), kind=kLoop, calls=%fused_computation.1 | loop fusion | flops 22413312 | bytes 22413312 | tf_op jit(solution)/shard_map/concatenate | solution.py:73
  23.8 8.6 %all-to-all-start = ((bf16[32,24,7296]{2,1,0:T(8,128)(2,1)}), bf16[32,24,7296]{2,1,0:T(8,128)(2,1)}, u32[]{:S(2)}, u32[]{:S(2)}) async-start(bf16[32,24,7296]{2,1,0:T(8,128)(2,1)} %pad_maximum_fusion), calls=%async_computation | async-start | bytes 22413312 | tf_op jit(solution)/shard_map/all_to_all | solution.py:80
  32.5 0.7 all-gather.2.cloned.1.call-update
  33.2 3.5 fusion.43
  36.8 1.6 collective-permute-start.3
  38.4 2.1 collective-permute-start.4
  40.5 2.7 collective-permute-start.1
  43.2 4.1 squeeze.35.clone.1
  47.3 1.5 bitcast_dynamic-update-slice_fusion.3
  49.7 59.5 %collective-permute-done.3 = bf16[1,2,3584,128]{3,2,1,0:T(8,128)(2,1)} collective-permute-done((bf16[1,2,3584,128]{3,2,1,0:T(8,128)(2,1)}, bf16[1,2,3584,128]{3,2,1,0:T(8,128)(2,1)}, u32[]{:S(2)}, u32[]{:S(2)}) %collective-permute-start.3) | collective-permute-done | bytes 1835040 | tf_op jit(solution)/shard_map/ppermute | solution.py:23
  109.2 70.0 %collective-permute-done = bf16[1,2,3584,128]{3,2,1,0:T(8,128)(2,1)} collective-permute-done((bf16[1,2,3584,128]{3,2,1,0:T(8,128)(2,1)S(1)}, bf16[1,2,3584,128]{3,2,1,0:T(8,128)(2,1)}, u32[]{:S(2)}, u32[]{:S(2)}) %collective-permute-start) | collective-permute-done | bytes 1835040 | tf_op jit(solution)/shard_map/ppermute | solution.py:23
  179.7 3.0 bitcast_dynamic-update-slice_fusion.2
  182.7 2.9 bitcast_dynamic-update-slice_fusion.1
  185.6 32.8 %collective-permute-done.5 = bf16[1,2,3584,128]{3,2,1,0:T(8,128)(2,1)S(1)} collective-permute-done((bf16[1,2,3584,128]{3,2,1,0:T(8,128)(2,1)}, bf16[1,2,3584,128]{3,2,1,0:T(8,128)(2,1)S(1)}, u32[]{:S(2)}, u32[]{:S(2)}) %collective-permute-start.5) | collective-permute-done | bytes 1835040 | tf_op jit(solution)/shard_map/ppermute | solution.py:23
  218.4 1.4 bitcast_dynamic-update-slice_fusion
  219.8 1.1 convert_reduce_fusion.2
  220.9 7.9 %fusion.14 = f32[768,512]{0,1:T(8,128)} fusion(bf16[768,7296]{1,0:T(8,128)(2,1)} %bitcast.3, bf16[2,3584,512]{2,1,0:T(8,128)(2,1)} %bitcast_dynamic-update-slice_fusion), kind=kOutput, calls=%fused_computation.28 | convolution fusion | flops 2818572288 | bytes 10747904 | tf_op jit(solution)/shard_map/dot_general | solution.py:95
  228.8 9.8 %fusion.2 = f32[768,4,2,128]{0,3,2,1:T(8,128)S(1)} fusion(bf16[4,2,128,3584]{3,2,1,0:T(8,128)(2,1)} %bitcast.104, bf16[768,7296]{1,0:T(8,128)(2,1)} %bitcast.3), kind=kOutput, calls=%fused_computation.9 | convolution fusion | flops 5637144576 | bytes 15990784 | tf_op jit(solution)/shard_map/dot_general | solution.py:34
  238.8 1.2 copy-done.8
  240.0 8.6 %fusion.27 = (f32[768]{0:T(1024)S(1)}, bf16[768,512]{0,1:T(8,128)(2,1)S(1)}, bf16[768,512]{0,1:T(8,128)(2,1)}, bf16[768,512]{0,1:T(8,128)(2,1)}) fusion(f32[768,4,1,128]{0,3,2,1:T(8,128)S(1)} %get-tuple-element.57, f32[768,512]{0,1:T(8,128)S(1)} %copy-done.8, f32[768]{0:T(1024)S(1)} %convert_reduce_fusion.2, ...), kind=kOutput, calls=%fused_computation.52 | convolution fusion | flops 2826042624 | bytes 14686208 | tf_op jit(solution)/shard_map/dot_general | solution.py:96
  248.6 7.6 %convolution_convert_fusion.1 = bf16[512,3584]{1,0:T(8,128)(2,1)} fusion(bf16[768,512]{0,1:T(8,128)(2,1)S(1)} %get-tuple-element.45, f32[768]{0:T(1024)S(1)} %convert_reduce_fusion.2, bf16[768,7296]{1,0:T(8,128)(2,1)} %bitcast.3), kind=kOutput, calls=%fused_computation.4 | convolution fusion | flops 2828664832 | bytes 9964544 | tf_op jit(solution)/shard_map/dot_general | solution.py:40
  256.4 3.0 bitcast_dynamic-update-slice_fusion.6
  259.4 3.0 bitcast_dynamic-update-slice_fusion.5
  262.4 2.9 bitcast_dynamic-update-slice_fusion.4
  265.3 7.6 %fusion.18 = f32[768,512]{0,1:T(8,128)S(1)} fusion(bf16[768,7296]{1,0:T(8,128)(2,1)} %bitcast.3, bf16[2,3584,512]{2,1,0:T(8,128)(2,1)} %bitcast_dynamic-update-slice_fusion.4), kind=kOutput, calls=%fused_computation.32 | convolution fusion | flops 2818572288 | bytes 10747904 | tf_op jit(solution)/shard_map/dot_general | solution.py:95
  272.9 6.5 %fusion.28 = (f32[768]{0:T(1024)S(1)}, bf16[768,512]{0,1:T(8,128)(2,1)S(1)}, bf16[768,512]{0,1:T(8,128)(2,1)S(1)}, bf16[768,512]{0,1:T(8,128)(2,1)S(1)}) fusion(f32[768,4,1,128]{0,3,2,1:T(8,128)S(1)} %get-tuple-element.58, f32[768,512]{0,1:T(8,128)S(1)} %fusion.18, f32[768]{0:T(1024)S(1)} %convert_reduce_fusion.2, bf16[2,3584,512]{2,1,0:T(8,128)(2,1)S(1)} %copy-done.3, ...), kind=kOutput, calls=%fused_computation.55 | convolution fusion | flops 2826042624 | bytes 14687232 | tf_op jit(solution)/shard_map/dot_general | solution.py:96
  279.4 6.0 %fusion.22 = f32[768,3584]{1,0:T(8,128)} fusion(bf16[768,512]{0,1:T(8,128)(2,1)S(1)} %get-tuple-element.56, bf16[2,3584,512]{2,1,0:T(8,128)(2,1)S(1)} %copy-done.3), kind=kOutput, calls=%fused_computation.36 | convolution fusion | flops 2818572288 | bytes 15466496 | tf_op jit(solution)/shard_map/dot_general | solution.py:34
  285.4 5.8 %fusion.23 = f32[768,3584]{1,0:T(8,128)} fusion(bf16[768,512]{0,1:T(8,128)(2,1)S(1)} %get-tuple-element.48, bf16[2,3584,512]{2,1,0:T(8,128)(2,1)S(1)} %copy-done.3), kind=kOutput, calls=%fused_computation.37 | convolution fusion | flops 2818572288 | bytes 15466496 | tf_op jit(solution)/shard_map/dot_general | solution.py:34
  291.1 7.9 %fusion.24 = f32[768,3584]{1,0:T(8,128)} fusion(bf16[768,512]{0,1:T(8,128)(2,1)S(1)} %copy-done.7, bf16[2,3584,512]{2,1,0:T(8,128)(2,1)} %bitcast_dynamic-update-slice_fusion), kind=kOutput, calls=%fused_computation.38 | convolution fusion | flops 2818572288 | bytes 15466496 | tf_op jit(solution)/shard_map/dot_general | solution.py:34
  299.0 7.6 %convolution_convert_fusion.2 = bf16[512,3584]{1,0:T(8,128)(2,1)} fusion(bf16[768,512]{0,1:T(8,128)(2,1)S(1)} %get-tuple-element.47, f32[768]{0:T(1024)S(1)} %convert_reduce_fusion.2, bf16[768,7296]{1,0:T(8,128)(2,1)} %bitcast.3), kind=kOutput, calls=%fused_computation.5 | convolution fusion | flops 2828664832 | bytes 9964544 | tf_op jit(solution)/shard_map/dot_general | solution.py:40
  306.7 1.1 copy-done.5
  307.8 16.7 %add_convert_fusion = bf16[768,3584]{1,0:T(8,128)(2,1)} fusion(f32[768,3584]{1,0:T(8,128)} %fusion.24, f32[768,3584]{1,0:T(8,128)} %fusion.23, f32[768,3584]{1,0:T(8,128)} %fusion.22, bf16[768,512]{0,1:T(8,128)(2,1)S(1)} %copy-done.5, bf16[2,3584,512]{2,1,0:T(8,128)(2,1)} %bitcast_dynamic-update-slice_fusion), kind=kOutput, calls=%fused_computation.3 | convolution fusion | flops 2829582336 | bytes 42991616 | tf_op jit(solution)/shard_map/dot_general | solution.py:34
  324.5 0.6 select_convert_fusion
  325.3 3.0 pad_maximum_fusion.1
  328.4 74.9 %all_to_all.10 = bf16[32,24,3712]{2,1,0:T(8,128)(2,1)S(1)} all-to-all(bf16[32,24,3712]{2,1,0:T(8,128)(2,1)S(1)} %pad_maximum_fusion.1), channel_id=1, replica_groups=mesh['expert'=32,'dp'=4] {'expert'}, dimensions={0} | all-to-all | bytes 11403264 | tf_op jit(solution)/shard_map/all_to_all | solution.py:120
  403.3 2.5 copy-done.4
  406.5 0.6 multiply_divide_fusion
  407.1 4.4 %fusion.5 = bf16[64,3584]{1,0:T(8,128)(2,1)} fusion(bf16[768,3712]{1,0:T(8,128)(2,1)} %bitcast.99, bf16[768,64]{0,1:T(8,128)(2,1)S(1)} %convert_reduce_fusion), kind=kOutput, calls=%fused_computation.15 | convolution fusion | flops 352550912 | bytes 6062080 | tf_op jit(solution)/shard_map/dot_general | solution.py:40
  411.5 7.8 %fusion.26 = (bf16[1,256,3584]{2,1,0:T(8,128)(2,1)}, bf16[1,256,3584]{2,1,0:T(8,128)(2,1)}, bf16[1,256,3584]{2,1,0:T(8,128)(2,1)}) fusion(bf16[1,256,3584]{2,1,0:T(8,128)(2,1)} %param.19, bf16[1,128,3584]{2,1,0:T(8,128)(2,1)} %bitcast.100, bf16[1,128,3584]{2,1,0:T(8,128)(2,1)} %bitcast.101, bf16[1,256,3584]{2,1,0:T(8,128)(2,1)} %param.18, ...), kind=kLoop, calls=%fused_computation.40 | loop fusion | flops 23855104 | bytes 12845056 | tf_op jit(solution)/shard_map/convert_element_type | solution.py:142
  (57 shorter events, 4.3 us)
Async XLA Ops:
  23.8 196.0 %all-to-all-start = ((bf16[32,24,7296]{2,1,0:T(8,128)(2,1)}), bf16[32,24,7296]{2,1,0:T(8,128)(2,1)}, u32[]{:S(2)}, u32[]{:S(2)}) async-start(bf16[32,24,7296]{2,1,0:T(8,128)(2,1)} %pad_maximum_fusion), calls=%async_computation | async-start | bytes 22413312 | tf_op jit(solution)/shard_map/all_to_all | solution.py:80
  32.4 196.3 %all-gather.2.cloned.1.call-start = ((), (), s32[]{:S(2)}) async-start(), calls=%async_computation.4 | async-start | bytes 9175040 | tf_op jit(solution)/shard_map/all_gather | solution.py:75
  33.2 378.3 %reduce-scatter.5.cloned.1.call-start = ((), (), s32[]{:S(2)}) async-start(), calls=%async_computation.6 | async-start | bytes 4587520 | tf_op jit(solution)/shard_map/reduce_scatter | solution.py:103
  36.8 72.4 %collective-permute-start.3 = (bf16[1,2,3584,128]{3,2,1,0:T(8,128)(2,1)}, bf16[1,2,3584,128]{3,2,1,0:T(8,128)(2,1)}, u32[]{:S(2)}, u32[]{:S(2)}) collective-permute-start(bf16[1,2,3584,128]{3,2,1,0:T(8,128)(2,1)} %get-tuple-element.53), channel_id=1, source_target_pairs={{0,1},{1,2},{2,3},{3,0},{4,5},{5,6},{6,7},{7,4},{8,9},{9,10},{10,1... | collective-permute-start | bytes 5505032 | tf_op jit(solution)/shard_map/ppermute | solution.py:23
  38.4 144.3 %collective-permute-start.4 = (bf16[1,2,3584,128]{3,2,1,0:T(8,128)(2,1)}, bf16[1,2,3584,128]{3,2,1,0:T(8,128)(2,1)}, u32[]{:S(2)}, u32[]{:S(2)}) collective-permute-start(bf16[1,2,3584,128]{3,2,1,0:T(8,128)(2,1)} %get-tuple-element.53), channel_id=1, source_target_pairs={{0,3},{1,0},{2,1},{3,2},{4,7},{5,4},{6,5},{7,6},{8,11},{9,8},{10,9... | collective-permute-start | bytes 5505032 | tf_op jit(solution)/shard_map/ppermute | solution.py:26
  40.5 138.7 %collective-permute-start = (bf16[1,2,3584,128]{3,2,1,0:T(8,128)(2,1)S(1)}, bf16[1,2,3584,128]{3,2,1,0:T(8,128)(2,1)}, u32[]{:S(2)}, u32[]{:S(2)}) collective-permute-start(bf16[1,2,3584,128]{3,2,1,0:T(8,128)(2,1)S(1)} %get-tuple-element.54), channel_id=1, source_target_pairs={{0,1},{1,2},{2,3},{3,0},{4,5},{5,6},{6,7},{7,4},{8,9},{9,10},{10,1... | collective-permute-start | bytes 5505032 | tf_op jit(solution)/shard_map/ppermute | solution.py:23
  40.5 218.9 %collective-permute-start.1 = (bf16[1,2,3584,128]{3,2,1,0:T(8,128)(2,1)S(1)}, bf16[1,2,3584,128]{3,2,1,0:T(8,128)(2,1)}, u32[]{:S(2)}, u32[]{:S(2)}) collective-permute-start(bf16[1,2,3584,128]{3,2,1,0:T(8,128)(2,1)S(1)} %get-tuple-element.54), channel_id=1, source_target_pairs={{0,3},{1,0},{2,1},{3,2},{4,7},{5,4},{6,5},{7,6},{8,11},{9,8},{10,9... | collective-permute-start | bytes 5505032 | tf_op jit(solution)/shard_map/ppermute | solution.py:26
  43.2 4.1 copy-start
  49.7 135.9 %copy-start.2 = (bf16[2,3584,512]{2,1,0:T(8,128)(2,1)}, bf16[2,3584,512]{2,1,0:T(8,128)(2,1)S(1)}, u32[]{:S(2)}) copy-start(bf16[2,3584,512]{2,1,0:T(8,128)(2,1)S(1)} %bitcast_dynamic-update-slice_fusion.7) | copy-start | bytes 22020100
  109.2 109.2 %collective-permute-start.5 = (bf16[1,2,3584,128]{3,2,1,0:T(8,128)(2,1)}, bf16[1,2,3584,128]{3,2,1,0:T(8,128)(2,1)S(1)}, u32[]{:S(2)}, u32[]{:S(2)}) collective-permute-start(bf16[1,2,3584,128]{3,2,1,0:T(8,128)(2,1)} %collective-permute-done.3), channel_id=1, source_target_pairs={{0,1},{1,2},{2,3},{3,0},{4,5},{5,6},{6,7},{7,4},{8,9},{9,10},{10,1... | collective-permute-start | bytes 5505032 | tf_op jit(solution)/shard_map/ppermute | solution.py:23
  179.2 83.2 %collective-permute-start.2 = (bf16[1,2,3584,128]{3,2,1,0:T(8,128)(2,1)}, bf16[1,2,3584,128]{3,2,1,0:T(8,128)(2,1)}, u32[]{:S(2)}, u32[]{:S(2)}) collective-permute-start(bf16[1,2,3584,128]{3,2,1,0:T(8,128)(2,1)} %collective-permute-done), channel_id=1, source_target_pairs={{0,1},{1,2},{2,3},{3,0},{4,5},{5,6},{6,7},{7,4},{8,9},{9,10},{10,1... | collective-permute-start | bytes 5505032 | tf_op jit(solution)/shard_map/ppermute | solution.py:23
  238.6 1.4 copy-start.8
  256.2 155.3 %reduce-scatter.3.cloned.1.call-start = ((), (), s32[]{:S(2)}) async-start(), calls=%async_computation.5 | async-start | bytes 4587520 | tf_op jit(solution)/shard_map/reduce_scatter | solution.py:103
  265.3 7.6 %copy-start.3 = (bf16[2,3584,512]{2,1,0:T(8,128)(2,1)S(1)}, bf16[2,3584,512]{2,1,0:T(8,128)(2,1)}, u32[]{:S(2)}) copy-start(bf16[2,3584,512]{2,1,0:T(8,128)(2,1)} %bitcast_dynamic-update-slice_fusion.4) | copy-start | bytes 22020100
  285.4 5.8 %copy-start.7 = (bf16[768,512]{0,1:T(8,128)(2,1)S(1)}, bf16[768,512]{0,1:T(8,128)(2,1)}, u32[]{:S(2)}) copy-start(bf16[768,512]{0,1:T(8,128)(2,1)} %get-tuple-element.49) | copy-start | bytes 2359300
  306.7 1.1 copy-start.5
  328.4 78.1 %copy-start.6 = (f32[64,8]{0,1:T(8,128)S(1)}, f32[64,8]{0,1:T(8,128)}, u32[]{:S(2)}) copy-start(f32[64,8]{0,1:T(8,128)} %param.15) | copy-start | bytes 6148
  403.3 2.6 copy-start.4
  403.3 8.2 %copy-start.1 = (bf16[1,256,3584]{2,1,0:T(8,128)(2,1)S(1)}, bf16[1,256,3584]{2,1,0:T(8,128)(2,1)}, u32[]{:S(2)}) copy-start(bf16[1,256,3584]{2,1,0:T(8,128)(2,1)} %param.17) | copy-start | bytes 5505028
Sparse Core Ops, SparseCore 0:
  34.9 135.6 all-gather.1
  256.3 43.7 reduce-scatter.4
  306.8 43.7 reduce-scatter.2
